TPU v7x, 32 devices: a whole 2x2x4 slice. The times are simulated.
32 devices in a mesh: gx: 8 (over y, x, core), gy: 4 (over z).
Axes of the slice: x: 2, y: 2, z: 4, core: 2. Of those that a mesh axis runs over, the one named last changes fastest.
Arguments:
- prior_gas_warmth: float32 [128, 128, 512], P(None, 'gx', 'gy'), may hold values from -8 to 8
- fire_power_output: float32 [128, 128, 512], P(None, 'gx', 'gy'), may hold values from -6 to 6
- measured_warmth: float32 [32768], P(('gx', 'gy')), may hold values from -8 to 8
- reading_noise_spread: float32 [32768], P(('gx', 'gy')), may hold values from 1.15 to 6
- reading_local_location: int32 [32768], P(('gx', 'gy')), may hold values from 0 to 2047
Outputs:
- temperature_analysis: float32 [128, 128, 512], P(None, 'gx', 'gy')
- heat_analysis: float32 [128, 128, 512], P(None, 'gx', 'gy')
All inputs are finite; a program needn't handle non-finite values.
Results may differ from a plain program's by a relative error of at most 0.0003.
Values sent between devices are 32-bit elements; how exact they have to be, the bound alone decides.
No kernel may reach another device: no remote copies, remote signals or barrier semaphores. Data moves between devices by JAX's collectives and lax.ppermute only.
A program may use at most 64 MiB of HBM per device.

v0:
```python
import math
import jax
import jax.numpy as jnp
from jax import lax
from jax.sharding import PartitionSpec as P

diffusion = 0.2
heating = 0.5


def with_halo(block, sides, width):
    for axis, dim in sides:
        count = lax.axis_size(axis)
        forward = [(i, i + 1) for i in range(count - 1)]
        backward = [(target, source) for source, target in forward]
        low = lax.ppermute(
            lax.slice_in_dim(block, block.shape[dim] - width, None, axis=dim), axis, forward
        )
        high = lax.ppermute(lax.slice_in_dim(block, 0, width, axis=dim), axis, backward)
        block = jnp.concatenate([low, block, high], axis=dim)
    return block


def propagate_model(padded_field, source_term):
    laplacian = (
        padded_field[:, 2:, 1:-1]
        + padded_field[:, :-2, 1:-1]
        + padded_field[:, 1:-1, 2:]
        + padded_field[:, 1:-1, :-2]
        - 4.0 * padded_field[:, 1:-1, 1:-1]
    )
    return padded_field[:, 1:-1, 1:-1] + diffusion * laplacian + heating * source_term


def shards(
    prior_gas_warmth,
    fire_power_output,
    measured_warmth,
    reading_noise_spread,
    reading_local_location,
):
    sample_number, block_height_number, block_width_number = prior_gas_warmth.shape
    devices_all = lax.axis_size(("gx", "gy"))
    predicted_vector = prior_gas_warmth
    for section in range(2):
        bordered_vector = with_halo(predicted_vector, (("gx", 1), ("gy", 2)), 1)
        predicted_vector = propagate_model(bordered_vector, fire_power_output)
    grid_points_number = block_height_number * block_width_number
    warmth_vectorised = predicted_vector.reshape(sample_number, grid_points_number)
    heat_flat = fire_power_output.reshape(sample_number, grid_points_number)
    average_gas_warmth = jnp.mean(warmth_vectorised, axis=0)
    mean_heat = jnp.mean(heat_flat, axis=0)
    sample_deviation_matrix = warmth_vectorised - average_gas_warmth
    heat_anomaly = heat_flat - mean_heat
    picked = jnp.take(sample_deviation_matrix, reading_local_location, axis=1)
    coefficient_line = 1.0 / (reading_noise_spread * math.sqrt(sample_number - 1))
    s_matrix = picked * coefficient_line
    measurement_residual = (
        measured_warmth - jnp.take(average_gas_warmth, reading_local_location)
    ) * coefficient_line
    identity = jnp.eye(sample_number, dtype=jnp.float32)
    gram_local = (
        jnp.dot(s_matrix, s_matrix.T, precision=lax.Precision.HIGHEST) + identity / devices_all
    )
    projected = jnp.dot(s_matrix, measurement_residual, precision=lax.Precision.HIGHEST)
    gram_sum, projected_sum = lax.psum((gram_local, projected), ("gx", "gy"))
    lower = jnp.linalg.cholesky(gram_sum)
    mean_weights = jax.scipy.linalg.cho_solve((lower, True), projected_sum)
    inverse_factor = jax.scipy.linalg.solve_triangular(lower, identity, lower=True, trans=1)
    combination_matrix = mean_weights[:, None] + inverse_factor
    updated_warmth = average_gas_warmth + jnp.dot(
        combination_matrix.T, sample_deviation_matrix, precision=lax.Precision.HIGHEST
    )
    heat_out = mean_heat + jnp.dot(
        combination_matrix.T, heat_anomaly, precision=lax.Precision.HIGHEST
    )
    return (
        updated_warmth.reshape(sample_number, block_height_number, block_width_number),
        heat_out.reshape(sample_number, block_height_number, block_width_number),
    )


def solution(mesh):
    placed = (
        P(None, "gx", "gy"),
        P(None, "gx", "gy"),
        P(("gx", "gy")),
        P(("gx", "gy")),
        P(("gx", "gy")),
    )
    return jax.shard_map(
        shards,
        mesh=mesh,
        in_specs=placed,
        out_specs=(P(None, "gx", "gy"), P(None, "gx", "gy")),
        check_vma=False,
    )
```

profile of v0, /device:TPU:1, one launch (start us, length us, event | category | flops | bytes accessed | tf_op | source)
XLA Modules:
  0.0 214.9 jit_solution(14382763396117944814)
XLA Ops:
  7.2 0.0 all-reduce.2.cloned.1.call-start
  7.2 1.8 copy.128
  9.1 0.0 copy-start
  9.1 0.1 fusion.37
  9.2 2.1 collective-permute-start
  11.3 4.5 %collective-permute-start.1 = (f32[128,1,128]{0,1,2:T(1,128)S(1)}, f32[128,1,128]{0,1,2:T(1,128)S(1)}, u32[]{:S(2)}, u32[]{:S(2)}) collective-permute-start(f32[128,1,128]{0,1,2:T(1,128)S(1)} %get-tuple-element.12), channel_id=1, source_target_pairs={{0,4},{4,8},{8,12},{12,16},{16,20},{20,24},{24,28},{1,5},{5,9},{9,... | collective-permute-start | bytes 196616 | tf_op jit(solution)/shard_map/ppermute | solution.py:16
  15.8 0.0 collective-permute-done
  15.8 1.3 collective-permute-done.1
  17.1 1.3 collective-permute-start.2
  18.4 4.0 %collective-permute-start.3 = (f32[128,18,1]{0,1,2:T(8,128)S(1)}, f32[128,18,1]{0,1,2:T(8,128)S(1)}, u32[]{:S(2)}, u32[]{:S(2)}) collective-permute-start(f32[128,18,1]{0,1,2:T(8,128)S(1)} %get-tuple-element.9), channel_id=1, source_target_pairs={{0,1},{1,2},{2,3},{4,5},{5,6},{6,7},{8,9},{9,10},{10,11},{12,13},{... | collective-permute-start | bytes 27656 | tf_op jit(solution)/shard_map/ppermute | solution.py:16
  22.4 0.0 copy-done
  22.4 0.7 copy.129
  23.1 0.1 reduce_sum.19
  23.2 0.0 collective-permute-done.2
  23.2 0.0 collective-permute-done.3
  23.2 0.6 fusion.14
  23.8 0.1 fusion.36
  23.9 1.9 collective-permute-start.4
  25.9 5.3 %collective-permute-start.5 = (f32[128,1,128]{0,1,2:T(1,128)S(1)}, f32[128,1,128]{0,1,2:T(1,128)S(1)}, u32[]{:S(2)}, u32[]{:S(2)}) collective-permute-start(f32[128,1,128]{0,1,2:T(1,128)S(1)} %get-tuple-element.10), channel_id=1, source_target_pairs={{0,4},{4,8},{8,12},{12,16},{16,20},{20,24},{24,28},{1,5},{5,9},{9,... | collective-permute-start | bytes 196616 | tf_op jit(solution)/shard_map/ppermute | solution.py:16
  31.2 0.0 collective-permute-done.4
  31.2 1.3 collective-permute-done.5
  32.5 0.0 copy-start.4
  32.5 1.3 collective-permute-start.6
  33.8 4.5 %collective-permute-start.7 = (f32[128,18,1]{0,1,2:T(8,128)S(1)}, f32[128,18,1]{0,1,2:T(8,128)S(1)}, u32[]{:S(2)}, u32[]{:S(2)}) collective-permute-start(f32[128,18,1]{0,1,2:T(8,128)S(1)} %get-tuple-element.7), channel_id=1, source_target_pairs={{0,1},{1,2},{2,3},{4,5},{5,6},{6,7},{8,9},{9,10},{10,11},{12,13},{... | collective-permute-start | bytes 27656 | tf_op jit(solution)/shard_map/ppermute | solution.py:16
  38.4 0.0 copy-done.4
  38.4 0.0 collective-permute-done.6
  38.4 0.8 collective-permute-done.7
  39.2 0.7 fusion.34
  39.9 0.7 copy.131
  40.6 0.0 copy-start.1
  40.6 0.1 copy.130
  40.7 0.9 copy-done.1
  41.6 0.4 bitcast_subtract_fusion.2
  41.9 0.3 copy.132
  42.3 6.2 %gather_fusion.1 = f32[1024]{0:T(1024)S(1)} fusion(f32[2048]{0:T(1024)S(1)} %multiply_bitcast_fusion.1, s32[1024]{0:T(1024)S(1)} %fusion.30), kind=kCustom, calls=%fused_computation.1 | custom fusion | bytes 12288 | tf_op jit(solution)/shard_map/jit(_take)/gather | solution.py:59
  48.4 0.0 copy-start.5
  48.5 0.0 copy-start.6
  48.5 2.8 %gather_fusion = f32[1024,128]{1,0:T(8,128)S(1)} fusion(f32[128,2048]{0,1:T(8,128)S(1)} %copy.132, s32[1024]{0:T(1024)S(1)} %fusion.30), kind=kCustom, calls=%fused_computation | custom fusion | bytes 1052672 | tf_op jit(solution)/shard_map/jit(_take)/gather | solution.py:55
  51.3 0.0 copy-done.5
  51.3 0.0 copy-done.6
  51.3 0.0 copy-start.2
  51.3 2.3 %convolution_add_fusion.3 = f32[128,128]{1,0:T(8,128)} fusion(f32[1024,128]{1,0:T(8,128)S(1)} %gather_fusion, f32[1024]{0:T(1024)S(1)} %get-tuple-element.14, pred[1024]{0:T(1024)(128)(4,1)S(1)} %get-tuple-element.3), kind=kOutput, calls=%fused_computation.7 | convolution fusion | flops 201637888 | bytes 594944 | tf_op jit(solution)/shard_map/dot_general | solution.py:63
  53.6 0.0 all-reduce.2.cloned.1.call-update
  53.6 0.6 convolution_bitcast_fusion.2
  54.2 44.0 %psum.15 = f32[128]{0:T(128)S(1)} all-reduce(f32[128]{0:T(128)S(1)} %convolution_bitcast_fusion.2), channel_id=1, replica_groups=mesh['gx'=8,'gy'=4] {'gx','gy'}, use_global_device_ids=true, to_apply=%region_4.5 | all-reduce | flops 128 | bytes 1024 | tf_op jit(solution)/shard_map/psum | solution.py:66
  98.2 80.4 %all-reduce.2.cloned.1.call-done = f32[128,128]{1,0:T(8,128)} async-done(((f32[128,128]{1,0:T(8,128)}), f32[128,128]{1,0:T(8,128)}) %all-reduce.2.cloned.1.call-update) | async-done | bytes 65552 | tf_op jit(solution)/shard_map/psum | solution.py:66
  178.7 0.0 copy-start.3
  178.7 1.0 copy.133
  179.7 0.0 copy-done.3
  179.7 11.7 %cholesky.17 = f32[128,128]{1,0:T(8,128)S(1)} custom-call(f32[128,128]{1,0:T(8,128)S(1)} %fusion.29), custom_call_target="Cholesky" | custom-call | tf_op jit(solution)/shard_map/jit(cholesky)/cholesky | solution.py:67
  191.4 0.6 compare_reduce_fusion
  192.1 0.7 fusion.25
  192.7 9.8 %custom-call.13 = f32[1,128,128]{1,2,0:T(8,128)S(1)} custom-call(f32[1,128,128]{2,1,0:T(8,128)S(1)} %fusion.25), custom_call_target="InvertDiagBlocksLowerTriangular" | custom-call | tf_op jit(solution)/shard_map/jit(_cho_solve)/triangular_solve | solution.py:68
  202.6 0.2 convolution_bitcast_fusion.1
  202.7 0.2 convolution_bitcast_fusion
  202.9 0.2 convolution_add_fusion.2
  203.2 0.0 copy-done.2
  203.2 1.3 fusion
  204.5 1.3 fusion.1
  205.8 1.2 copy.137
  206.9 1.2 copy.135
  (8 shorter events, 0.1 us)
Async XLA Ops:
  7.2 171.5 %all-reduce.2.cloned.1.call-start = ((), (), s32[]{:S(2)}) async-start(), calls=%async_computation | async-start | bytes 131072 | tf_op jit(solution)/shard_map/psum | solution.py:66
  9.1 13.3 %copy-start = (f32[128,16,128]{2,1,0:T(8,128)S(1)}, f32[128,16,128]{2,1,0:T(8,128)}, u32[]{:S(2)}) copy-start(f32[128,16,128]{2,1,0:T(8,128)} %param.6) | copy-start | bytes 3145732
  9.2 6.6 %collective-permute-start = (f32[128,1,128]{0,1,2:T(1,128)S(1)}, f32[128,1,128]{0,1,2:T(1,128)S(1)}, u32[]{:S(2)}, u32[]{:S(2)}) collective-permute-start(f32[128,1,128]{0,1,2:T(1,128)S(1)} %get-tuple-element.13), channel_id=1, source_target_pairs={{4,0},{8,4},{12,8},{16,12},{20,16},{24,20},{28,24},{5,1},{9,5},{13... | collective-permute-start | bytes 196616 | tf_op jit(solution)/shard_map/ppermute | solution.py:19
  11.3 5.8 %collective-permute-start.1 = (f32[128,1,128]{0,1,2:T(1,128)S(1)}, f32[128,1,128]{0,1,2:T(1,128)S(1)}, u32[]{:S(2)}, u32[]{:S(2)}) collective-permute-start(f32[128,1,128]{0,1,2:T(1,128)S(1)} %get-tuple-element.12), channel_id=1, source_target_pairs={{0,4},{4,8},{8,12},{12,16},{16,20},{20,24},{24,28},{1,5},{5,9},{9,... | collective-permute-start | bytes 196616 | tf_op jit(solution)/shard_map/ppermute | solution.py:16
  17.1 6.1 %collective-permute-start.2 = (f32[128,18,1]{0,1,2:T(8,128)S(1)}, f32[128,18,1]{0,1,2:T(8,128)S(1)}, u32[]{:S(2)}, u32[]{:S(2)}) collective-permute-start(f32[128,18,1]{0,1,2:T(8,128)S(1)} %get-tuple-element.8), channel_id=1, source_target_pairs={{1,0},{2,1},{3,2},{5,4},{6,5},{7,6},{9,8},{10,9},{11,10},{13,12},{... | collective-permute-start | bytes 27656 | tf_op jit(solution)/shard_map/ppermute | solution.py:19
  18.4 4.9 %collective-permute-start.3 = (f32[128,18,1]{0,1,2:T(8,128)S(1)}, f32[128,18,1]{0,1,2:T(8,128)S(1)}, u32[]{:S(2)}, u32[]{:S(2)}) collective-permute-start(f32[128,18,1]{0,1,2:T(8,128)S(1)} %get-tuple-element.9), channel_id=1, source_target_pairs={{0,1},{1,2},{2,3},{4,5},{5,6},{6,7},{8,9},{9,10},{10,11},{12,13},{... | collective-permute-start | bytes 27656 | tf_op jit(solution)/shard_map/ppermute | solution.py:16
  23.9 7.3 %collective-permute-start.4 = (f32[128,1,128]{0,1,2:T(1,128)S(1)}, f32[128,1,128]{0,1,2:T(1,128)S(1)}, u32[]{:S(2)}, u32[]{:S(2)}) collective-permute-start(f32[128,1,128]{0,1,2:T(1,128)S(1)} %get-tuple-element.11), channel_id=1, source_target_pairs={{4,0},{8,4},{12,8},{16,12},{20,16},{24,20},{28,24},{5,1},{9,5},{13... | collective-permute-start | bytes 196616 | tf_op jit(solution)/shard_map/ppermute | solution.py:19
  25.9 6.7 %collective-permute-start.5 = (f32[128,1,128]{0,1,2:T(1,128)S(1)}, f32[128,1,128]{0,1,2:T(1,128)S(1)}, u32[]{:S(2)}, u32[]{:S(2)}) collective-permute-start(f32[128,1,128]{0,1,2:T(1,128)S(1)} %get-tuple-element.10), channel_id=1, source_target_pairs={{0,4},{4,8},{8,12},{12,16},{16,20},{20,24},{24,28},{1,5},{5,9},{9,... | collective-permute-start | bytes 196616 | tf_op jit(solution)/shard_map/ppermute | solution.py:16
  32.5 5.9 %copy-start.4 = (s32[1024]{0:T(1024)S(1)}, s32[1024]{0:T(1024)}, u32[]{:S(2)}) copy-start(s32[1024]{0:T(1024)} %param.9) | copy-start | bytes 12292
  32.5 5.9 %collective-permute-start.6 = (f32[128,18,1]{0,1,2:T(8,128)S(1)}, f32[128,18,1]{0,1,2:T(8,128)S(1)}, u32[]{:S(2)}, u32[]{:S(2)}) collective-permute-start(f32[128,18,1]{0,1,2:T(8,128)S(1)} %get-tuple-element.6), channel_id=1, source_target_pairs={{1,0},{2,1},{3,2},{5,4},{6,5},{7,6},{9,8},{10,9},{11,10},{13,12},{... | collective-permute-start | bytes 27656 | tf_op jit(solution)/shard_map/ppermute | solution.py:19
  33.8 5.4 %collective-permute-start.7 = (f32[128,18,1]{0,1,2:T(8,128)S(1)}, f32[128,18,1]{0,1,2:T(8,128)S(1)}, u32[]{:S(2)}, u32[]{:S(2)}) collective-permute-start(f32[128,18,1]{0,1,2:T(8,128)S(1)} %get-tuple-element.7), channel_id=1, source_target_pairs={{0,1},{1,2},{2,3},{4,5},{5,6},{6,7},{8,9},{9,10},{10,11},{12,13},{... | collective-permute-start | bytes 27656 | tf_op jit(solution)/shard_map/ppermute | solution.py:16
  40.6 1.0 copy-start.1
  48.4 2.8 %copy-start.5 = (f32[1024]{0:T(1024)S(1)}, f32[1024]{0:T(1024)}, u32[]{:S(2)}) copy-start(f32[1024]{0:T(1024)} %param.7) | copy-start | bytes 12292
  48.5 2.8 %copy-start.6 = (f32[1024]{0:T(1024)S(1)}, f32[1024]{0:T(1024)}, u32[]{:S(2)}) copy-start(f32[1024]{0:T(1024)} %param.8) | copy-start | bytes 12292
  51.3 151.8 %copy-start.2 = (f32[128,16,128]{2,1,0:T(8,128)S(1)}, f32[128,16,128]{2,1,0:T(8,128)}, u32[]{:S(2)}) copy-start(f32[128,16,128]{2,1,0:T(8,128)} %copy-done.1) | copy-start | bytes 3145732
  178.7 1.0 copy-start.3
Sparse Core Ops, SparseCore 0:
  53.7 124.8 all-reduce.1
where the time goes:
time: 215 us
  waiting for transfers between devices  83.8 us (39%)
  blocking collectives  44 us (20%)
  starting transfers between devices  25 us (12%)
  other arithmetic  24.7 us (11%)
  local copies, waits for them, and re-layouts  17 us (8%)
  between operations  14.4 us (7%)
  matrix products  6.05 us (3%)
    psum x1, waiting for transfers between devices, shards(): gram_sum, projected_sum = lax.psum((gram_local, projected), ('gx', 'gy'))  80.4 us
    psum x1, blocking collectives, shards(): gram_sum, projected_sum = lax.psum((gram_local, projected), ('gx', 'gy'))  44 us
    ppermute x4, starting transfers between devices, with_halo(): lax.ppermute(lax.slice_in_dim(block, block.shape[dim] - width, None, axis...  18.3 us
    another operation x3, other arithmetic, shards(): lower = jnp.linalg.cholesky(gram_sum)  12.4 us
    another operation x2, other arithmetic, shards(): mean_weights = jax.scipy.linalg.cho_solve((lower, True), projected_sum)  10.5 us
    ppermute x4, starting transfers between devices, with_halo(): lax.ppermute(lax.slice_in_dim(block, 0, width, axis=dim), axis, backward)  6.59 us
    gather x1, local copies, waits for them, and re-layouts, shards(): jnp.take(average_gas_warmth, reading_local_location)  6.15 us
    unnamed x18, local copies, waits for them, and re-layouts  5.79 us
  transfers between devices with their start and end apart: 9, of which 4 were waited for; matrix products, arithmetic and copies ran while one was open for 1% of the time, Pallas kernels for 0%

commit v1 on v0

--- a/solution.py
+++ b/solution.py
@@ -63,7 +63,7 @@
         jnp.dot(s_matrix, s_matrix.T, precision=lax.Precision.HIGHEST) + identity / devices_all
     )
     projected = jnp.dot(s_matrix, measurement_residual, precision=lax.Precision.HIGHEST)
-    gram_sum, projected_sum = lax.psum((gram_local, projected), ("gx", "gy"))
+    gram_sum, projected_sum = lax.psum(lax.psum((gram_local, projected), "gy"), "gx")
     lower = jnp.linalg.cholesky(gram_sum)
     mean_weights = jax.scipy.linalg.cho_solve((lower, True), projected_sum)
     inverse_factor = jax.scipy.linalg.solve_triangular(lower, identity, lower=True, trans=1)

time: 215 us -> 188 us (0.87)
  blocking collectives: 44 us -> 24.4 us
  waiting for transfers between devices: 83.8 us -> 72.8 us
    psum x1 -> x2, blocking collectives: 44 us -> 24.4 us  [the longest x1 15.8 us: shards(): lax.psum(lax.psum((gram_local, projected), 'gy'), 'gx')]
    psum x1 -> x2, waiting for transfers between devices: 80.4 us -> 69.4 us  [the longest x1 37.7 us: shards(): lax.psum((gram_local, projected), 'gy')]
  transfers between devices with their start and end apart: 9 -> 10, of which waited for: 4 -> 6; matrix products, arithmetic and copies ran while one was open for 1% -> 1% of each run, Pallas kernels for 0% -> 0%
where the time goes in v1:
time: 188 us; the launch traced here: 186 us
  waiting for transfers between devices  72.8 us (39%)
  other arithmetic  25.7 us (14%)
  starting transfers between devices  25.2 us (13%)
  blocking collectives  24.4 us (13%)
  local copies, waits for them, and re-layouts  17.3 us (9%)
  between operations  14.4 us (8%)
  matrix products  6.05 us (3%)
    psum x1, waiting for transfers between devices, shards(): lax.psum((gram_local, projected), 'gy')  37.7 us
    psum x1, waiting for transfers between devices, shards(): lax.psum(lax.psum((gram_local, projected), 'gy'), 'gx')  31.7 us
    ppermute x4, starting transfers between devices, with_halo(): lax.ppermute(lax.slice_in_dim(block, block.shape[dim] - width, None, axis...  18.4 us
    psum x1, blocking collectives, shards(): lax.psum(lax.psum((gram_local, projected), 'gy'), 'gx')  15.8 us
    another operation x3, other arithmetic, shards(): lower = jnp.linalg.cholesky(gram_sum)  12.4 us
    another operation x2, other arithmetic, shards(): mean_weights = jax.scipy.linalg.cho_solve((lower, True), projected_sum)  10.5 us
    psum x1, blocking collectives, shards(): lax.psum((gram_local, projected), 'gy')  8.62 us
    ppermute x4, starting transfers between devices, with_halo(): lax.ppermute(lax.slice_in_dim(block, 0, width, axis=dim), axis, backward)  6.72 us
  transfers between devices with their start and end apart: 10, of which 6 were waited for; matrix products, arithmetic and copies ran while one was open for 1% of the time, Pallas kernels for 0%

profile of v1, /device:TPU:1, one launch (start us, length us, event | category | flops | bytes accessed | tf_op | source)
XLA Modules:
  0.0 185.9 jit_solution(17168268564608249754)
XLA Ops:
  7.2 0.0 all-reduce.3.cloned.1.call-start
  7.2 1.8 copy.128
  9.1 0.0 copy-start
  9.1 0.1 fusion.37
  9.2 2.1 %collective-permute-start = (f32[128,1,128]{0,1,2:T(1,128)S(1)}, f32[128,1,128]{0,1,2:T(1,128)S(1)}, u32[]{:S(2)}, u32[]{:S(2)}) collective-permute-start(f32[128,1,128]{0,1,2:T(1,128)S(1)} %get-tuple-element.13), channel_id=1, source_target_pairs={{4,0},{8,4},{12,8},{16,12},{20,16},{24,20},{28,24},{5,1},{9,5},{13... | collective-permute-start | bytes 196616 | tf_op jit(solution)/shard_map/ppermute | solution.py:19
  11.3 4.5 %collective-permute-start.1 = (f32[128,1,128]{0,1,2:T(1,128)S(1)}, f32[128,1,128]{0,1,2:T(1,128)S(1)}, u32[]{:S(2)}, u32[]{:S(2)}) collective-permute-start(f32[128,1,128]{0,1,2:T(1,128)S(1)} %get-tuple-element.12), channel_id=1, source_target_pairs={{0,4},{4,8},{8,12},{12,16},{16,20},{20,24},{24,28},{1,5},{5,9},{9,... | collective-permute-start | bytes 196616 | tf_op jit(solution)/shard_map/ppermute | solution.py:16
  15.8 0.0 collective-permute-done
  15.8 1.3 collective-permute-done.1
  17.1 1.3 collective-permute-start.2
  18.4 4.0 %collective-permute-start.3 = (f32[128,18,1]{0,1,2:T(8,128)S(1)}, f32[128,18,1]{0,1,2:T(8,128)S(1)}, u32[]{:S(2)}, u32[]{:S(2)}) collective-permute-start(f32[128,18,1]{0,1,2:T(8,128)S(1)} %get-tuple-element.9), channel_id=1, source_target_pairs={{0,1},{1,2},{2,3},{4,5},{5,6},{6,7},{8,9},{9,10},{10,11},{12,13},{... | collective-permute-start | bytes 27656 | tf_op jit(solution)/shard_map/ppermute | solution.py:16
  22.4 0.0 copy-done
  22.4 0.7 copy.129
  23.1 0.0 collective-permute-done.2
  23.1 0.1 collective-permute-done.3
  23.2 0.6 fusion.14
  23.8 0.0 copy-start.1
  23.8 0.1 fusion.36
  23.9 2.1 %collective-permute-start.4 = (f32[128,1,128]{0,1,2:T(1,128)S(1)}, f32[128,1,128]{0,1,2:T(1,128)S(1)}, u32[]{:S(2)}, u32[]{:S(2)}) collective-permute-start(f32[128,1,128]{0,1,2:T(1,128)S(1)} %get-tuple-element.11), channel_id=1, source_target_pairs={{4,0},{8,4},{12,8},{16,12},{20,16},{24,20},{28,24},{5,1},{9,5},{13... | collective-permute-start | bytes 196616 | tf_op jit(solution)/shard_map/ppermute | solution.py:19
  26.0 5.4 %collective-permute-start.5 = (f32[128,1,128]{0,1,2:T(1,128)S(1)}, f32[128,1,128]{0,1,2:T(1,128)S(1)}, u32[]{:S(2)}, u32[]{:S(2)}) collective-permute-start(f32[128,1,128]{0,1,2:T(1,128)S(1)} %get-tuple-element.10), channel_id=1, source_target_pairs={{0,4},{4,8},{8,12},{12,16},{16,20},{20,24},{24,28},{1,5},{5,9},{9,... | collective-permute-start | bytes 196616 | tf_op jit(solution)/shard_map/ppermute | solution.py:16
  31.4 0.0 collective-permute-done.4
  31.4 1.3 collective-permute-done.5
  32.7 0.0 copy-start.4
  32.7 1.3 collective-permute-start.6
  34.0 4.5 %collective-permute-start.7 = (f32[128,18,1]{0,1,2:T(8,128)S(1)}, f32[128,18,1]{0,1,2:T(8,128)S(1)}, u32[]{:S(2)}, u32[]{:S(2)}) collective-permute-start(f32[128,18,1]{0,1,2:T(8,128)S(1)} %get-tuple-element.7), channel_id=1, source_target_pairs={{0,1},{1,2},{2,3},{4,5},{5,6},{6,7},{8,9},{9,10},{10,11},{12,13},{... | collective-permute-start | bytes 27656 | tf_op jit(solution)/shard_map/ppermute | solution.py:16
  38.6 0.0 copy-done.4
  38.6 0.0 copy-done.1
  38.6 0.1 reduce_sum.19
  38.7 0.0 collective-permute-done.6
  38.8 0.6 collective-permute-done.7
  39.4 0.7 fusion.34
  40.1 0.7 copy.131
  40.8 0.1 copy.130
  40.9 1.4 bitcast_subtract_fusion.2
  42.2 1.5 copy.132
  43.8 6.2 %gather_fusion.1 = f32[1024]{0:T(1024)S(1)} fusion(f32[2048]{0:T(1024)S(1)} %multiply_bitcast_fusion.1, s32[1024]{0:T(1024)S(1)} %fusion.30), kind=kCustom, calls=%fused_computation.1 | custom fusion | bytes 12288 | tf_op jit(solution)/shard_map/jit(_take)/gather | solution.py:59
  49.9 0.0 copy-start.5
  49.9 0.0 copy-start.6
  49.9 2.8 %gather_fusion = f32[1024,128]{1,0:T(8,128)S(1)} fusion(f32[128,2048]{0,1:T(8,128)S(1)} %copy.132, s32[1024]{0:T(1024)S(1)} %fusion.30), kind=kCustom, calls=%fused_computation | custom fusion | bytes 1052672 | tf_op jit(solution)/shard_map/jit(_take)/gather | solution.py:55
  52.8 0.0 copy-done.5
  52.8 0.0 copy-done.6
  52.8 2.3 %convolution_add_fusion.3 = f32[128,128]{1,0:T(8,128)} fusion(f32[1024,128]{1,0:T(8,128)S(1)} %gather_fusion, f32[1024]{0:T(1024)S(1)} %get-tuple-element.14, pred[1024]{0:T(1024)(128)(4,1)S(1)} %get-tuple-element.3), kind=kOutput, calls=%fused_computation.7 | convolution fusion | flops 201637888 | bytes 594944 | tf_op jit(solution)/shard_map/dot_general | solution.py:63
  55.1 0.0 all-reduce.3.cloned.1.call-update
  55.1 0.0 all-reduce.5.cloned.1.call-start
  55.2 37.7 %all-reduce.3.cloned.1.call-done = f32[128,128]{1,0:T(8,128)} async-done(((f32[128,128]{1,0:T(8,128)}), f32[128,128]{1,0:T(8,128)}) %all-reduce.3.cloned.1.call-update) | async-done | bytes 65552 | tf_op jit(solution)/shard_map/psum | solution.py:66
  92.8 0.0 all-reduce.5.cloned.1.call-update
  92.9 0.6 convolution_bitcast_fusion.2
  93.5 8.6 %psum.30 = f32[128]{0:T(128)S(1)} all-reduce(f32[128]{0:T(128)S(1)} %convolution_bitcast_fusion.2), channel_id=1, replica_groups=mesh['gx'=8,'gy'=4] {'gy'}, use_global_device_ids=true, to_apply=%region_5.6 | all-reduce | flops 128 | bytes 1024 | tf_op jit(solution)/shard_map/psum | solution.py:66
  102.1 15.8 %psum.31 = f32[128]{0:T(128)S(1)} all-reduce(f32[128]{0:T(128)S(1)} %psum.30), channel_id=1, replica_groups=mesh['gx'=8,'gy'=4] {'gx'}, use_global_device_ids=true, to_apply=%region_6.7 | all-reduce | flops 128 | bytes 1024 | tf_op jit(solution)/shard_map/psum | solution.py:66
  117.9 31.7 %all-reduce.5.cloned.1.call-done = f32[128,128]{1,0:T(8,128)} async-done(((f32[128,128]{1,0:T(8,128)}), f32[128,128]{1,0:T(8,128)}) %all-reduce.5.cloned.1.call-update) | async-done | bytes 65552 | tf_op jit(solution)/shard_map/psum | solution.py:66
  149.6 1.0 copy.133
  150.6 0.0 copy-done.3
  150.7 11.7 %cholesky.17 = f32[128,128]{1,0:T(8,128)S(1)} custom-call(f32[128,128]{1,0:T(8,128)S(1)} %fusion.29), custom_call_target="Cholesky" | custom-call | tf_op jit(solution)/shard_map/jit(cholesky)/cholesky | solution.py:67
  162.4 0.6 compare_reduce_fusion
  163.0 0.7 fusion.25
  163.7 9.8 %custom-call.13 = f32[1,128,128]{1,2,0:T(8,128)S(1)} custom-call(f32[1,128,128]{2,1,0:T(8,128)S(1)} %fusion.25), custom_call_target="InvertDiagBlocksLowerTriangular" | custom-call | tf_op jit(solution)/shard_map/jit(_cho_solve)/triangular_solve | solution.py:68
  173.5 0.2 convolution_bitcast_fusion.1
  173.7 0.2 convolution_bitcast_fusion
  173.9 0.2 convolution_add_fusion.2
  174.1 0.0 copy-start.2
  174.1 1.3 fusion
  175.4 0.0 copy-done.2
  175.4 1.3 fusion.1
  176.7 1.2 copy.137
  177.9 1.2 copy.135
  (9 shorter events, 0.1 us)
Async XLA Ops:
  7.2 85.7 %all-reduce.3.cloned.1.call-start = ((), (), s32[]{:S(2)}) async-start(), calls=%async_computation | async-start | bytes 131072 | tf_op jit(solution)/shard_map/psum | solution.py:66
  9.1 13.3 %copy-start = (f32[128,16,128]{2,1,0:T(8,128)S(1)}, f32[128,16,128]{2,1,0:T(8,128)}, u32[]{:S(2)}) copy-start(f32[128,16,128]{2,1,0:T(8,128)} %param.6) | copy-start | bytes 3145732
  9.2 6.6 %collective-permute-start = (f32[128,1,128]{0,1,2:T(1,128)S(1)}, f32[128,1,128]{0,1,2:T(1,128)S(1)}, u32[]{:S(2)}, u32[]{:S(2)}) collective-permute-start(f32[128,1,128]{0,1,2:T(1,128)S(1)} %get-tuple-element.13), channel_id=1, source_target_pairs={{4,0},{8,4},{12,8},{16,12},{20,16},{24,20},{28,24},{5,1},{9,5},{13... | collective-permute-start | bytes 196616 | tf_op jit(solution)/shard_map/ppermute | solution.py:19
  11.3 5.8 %collective-permute-start.1 = (f32[128,1,128]{0,1,2:T(1,128)S(1)}, f32[128,1,128]{0,1,2:T(1,128)S(1)}, u32[]{:S(2)}, u32[]{:S(2)}) collective-permute-start(f32[128,1,128]{0,1,2:T(1,128)S(1)} %get-tuple-element.12), channel_id=1, source_target_pairs={{0,4},{4,8},{8,12},{12,16},{16,20},{20,24},{24,28},{1,5},{5,9},{9,... | collective-permute-start | bytes 196616 | tf_op jit(solution)/shard_map/ppermute | solution.py:16
  17.1 6.0 %collective-permute-start.2 = (f32[128,18,1]{0,1,2:T(8,128)S(1)}, f32[128,18,1]{0,1,2:T(8,128)S(1)}, u32[]{:S(2)}, u32[]{:S(2)}) collective-permute-start(f32[128,18,1]{0,1,2:T(8,128)S(1)} %get-tuple-element.8), channel_id=1, source_target_pairs={{1,0},{2,1},{3,2},{5,4},{6,5},{7,6},{9,8},{10,9},{11,10},{13,12},{... | collective-permute-start | bytes 27656 | tf_op jit(solution)/shard_map/ppermute | solution.py:19
  18.4 4.8 %collective-permute-start.3 = (f32[128,18,1]{0,1,2:T(8,128)S(1)}, f32[128,18,1]{0,1,2:T(8,128)S(1)}, u32[]{:S(2)}, u32[]{:S(2)}) collective-permute-start(f32[128,18,1]{0,1,2:T(8,128)S(1)} %get-tuple-element.9), channel_id=1, source_target_pairs={{0,1},{1,2},{2,3},{4,5},{5,6},{6,7},{8,9},{9,10},{10,11},{12,13},{... | collective-permute-start | bytes 27656 | tf_op jit(solution)/shard_map/ppermute | solution.py:16
  23.8 14.8 %copy-start.1 = (f32[128,16,128]{2,1,0:T(8,128)S(1)}, f32[128,16,128]{2,1,0:T(8,128)}, u32[]{:S(2)}) copy-start(f32[128,16,128]{2,1,0:T(8,128)} %param.6) | copy-start | bytes 3145732
  23.9 7.5 %collective-permute-start.4 = (f32[128,1,128]{0,1,2:T(1,128)S(1)}, f32[128,1,128]{0,1,2:T(1,128)S(1)}, u32[]{:S(2)}, u32[]{:S(2)}) collective-permute-start(f32[128,1,128]{0,1,2:T(1,128)S(1)} %get-tuple-element.11), channel_id=1, source_target_pairs={{4,0},{8,4},{12,8},{16,12},{20,16},{24,20},{28,24},{5,1},{9,5},{13... | collective-permute-start | bytes 196616 | tf_op jit(solution)/shard_map/ppermute | solution.py:19
  26.0 6.7 %collective-permute-start.5 = (f32[128,1,128]{0,1,2:T(1,128)S(1)}, f32[128,1,128]{0,1,2:T(1,128)S(1)}, u32[]{:S(2)}, u32[]{:S(2)}) collective-permute-start(f32[128,1,128]{0,1,2:T(1,128)S(1)} %get-tuple-element.10), channel_id=1, source_target_pairs={{0,4},{4,8},{8,12},{12,16},{16,20},{20,24},{24,28},{1,5},{5,9},{9,... | collective-permute-start | bytes 196616 | tf_op jit(solution)/shard_map/ppermute | solution.py:16
  32.7 5.9 %copy-start.4 = (s32[1024]{0:T(1024)S(1)}, s32[1024]{0:T(1024)}, u32[]{:S(2)}) copy-start(s32[1024]{0:T(1024)} %param.9) | copy-start | bytes 12292
  32.7 6.0 %collective-permute-start.6 = (f32[128,18,1]{0,1,2:T(8,128)S(1)}, f32[128,18,1]{0,1,2:T(8,128)S(1)}, u32[]{:S(2)}, u32[]{:S(2)}) collective-permute-start(f32[128,18,1]{0,1,2:T(8,128)S(1)} %get-tuple-element.6), channel_id=1, source_target_pairs={{1,0},{2,1},{3,2},{5,4},{6,5},{7,6},{9,8},{10,9},{11,10},{13,12},{... | collective-permute-start | bytes 27656 | tf_op jit(solution)/shard_map/ppermute | solution.py:19
  34.0 5.4 %collective-permute-start.7 = (f32[128,18,1]{0,1,2:T(8,128)S(1)}, f32[128,18,1]{0,1,2:T(8,128)S(1)}, u32[]{:S(2)}, u32[]{:S(2)}) collective-permute-start(f32[128,18,1]{0,1,2:T(8,128)S(1)} %get-tuple-element.7), channel_id=1, source_target_pairs={{0,1},{1,2},{2,3},{4,5},{5,6},{6,7},{8,9},{9,10},{10,11},{12,13},{... | collective-permute-start | bytes 27656 | tf_op jit(solution)/shard_map/ppermute | solution.py:16
  49.9 2.9 %copy-start.5 = (f32[1024]{0:T(1024)S(1)}, f32[1024]{0:T(1024)}, u32[]{:S(2)}) copy-start(f32[1024]{0:T(1024)} %param.7) | copy-start | bytes 12292
  49.9 2.8 %copy-start.6 = (f32[1024]{0:T(1024)S(1)}, f32[1024]{0:T(1024)}, u32[]{:S(2)}) copy-start(f32[1024]{0:T(1024)} %param.8) | copy-start | bytes 12292
  55.1 94.5 %all-reduce.5.cloned.1.call-start = ((), (), s32[]{:S(2)}) async-start(), calls=%async_computation.1 | async-start | bytes 131072 | tf_op jit(solution)/shard_map/psum | solution.py:66
  149.6 1.0 copy-start.3
  174.1 1.3 copy-start.2
Sparse Core Ops, SparseCore 0:
  55.2 37.5 all-reduce.2
  96.2 53.3 all-reduce.4
